TPU v7x, 512 devices: a whole 4x4x16 slice. The times are simulated.
512 devices in a mesh: dp: 128 (over y, z, core), mp: 4 (over x).
Axes of the slice: x: 4, y: 4, z: 16, core: 2. Of those that a mesh axis runs over, the one named last changes fastest.
Arguments:
- points: float32 [262144, 256], P('dp'), may hold values from -28 to 28
- residual: float32 [128, 262144], P('mp', 'dp'), may hold values from -6 to 6
- coeffs: float32 [128, 262144], P('mp', 'dp'), may hold values from -4 to 4
- block_index: int32 [512], replicated, may hold values from 0 to 262143, as said below
Outputs:
- new_residual: float32 [128, 262144], P('mp', 'dp')
- new_coeffs: float32 [128, 262144], P('mp', 'dp')
Inputs may be any that keep to these rules, and one draw needn't show every extreme that they name: `block_index`: distinct example indices; the 2048 examples of one index of dp hold at most 16 of them, and those of some index hold exactly 16.
All inputs are finite; a program needn't handle non-finite values.
Results may differ from a plain program's by a relative error of at most 0.00018.
Values sent between devices are 32-bit elements; how exact they have to be, the bound alone decides.
No kernel may reach another device: no remote copies, remote signals or barrier semaphores. Data moves between devices by JAX's collectives and lax.ppermute only.
A program may use at most 64 MiB of HBM per device.

v0:
```python
import jax
import jax.numpy as jnp
from jax import lax
from jax.sharding import PartitionSpec as P

BLOCK = 512


ridge_weight = 1.0


def on_device(points, residual, coeffs, block_index):
    highest = lax.Precision.HIGHEST
    shard_rows = points.shape[0]
    feature_count = points.shape[1]
    output_rows = residual.shape[0]
    dp_count = lax.axis_size("dp")
    position = lax.axis_index("dp")
    owner_shard = block_index // shard_rows
    local_row = block_index - owner_shard * shard_rows
    mine = owner_shard == position
    safe_row = jnp.where(mine, local_row, 0)
    own_squares = jnp.sum(points * points, axis=1)
    square_total = lax.psum(jnp.sum(own_squares), "dp")
    mean_sq = square_total / (shard_rows * dp_count)
    picked_points = points[safe_row]
    picked_resid = residual[:, safe_row]
    slot_count = max(2, 4 * BLOCK // dp_count)
    same_owner = owner_shard[:, None] == owner_shard[None, :]
    earlier = lax.broadcasted_iota(jnp.int32, (BLOCK, BLOCK), 1) < lax.broadcasted_iota(
        jnp.int32, (BLOCK, BLOCK), 0
    )
    slot_rank = jnp.sum((same_owner & earlier).astype(jnp.int32), axis=1)
    slot_target = jnp.where(mine, slot_rank, slot_count)
    packed_points = (
        jnp.zeros((slot_count, feature_count), jnp.float32)
        .at[slot_target]
        .set(picked_points, mode="drop")
    )
    packed_resid = (
        jnp.zeros((output_rows, slot_count), jnp.float32)
        .at[:, slot_target]
        .set(picked_resid, mode="drop")
    )
    all_points, all_resid = (
        lax.all_gather(packed_points, "dp", axis=0, tiled=True),
        lax.all_gather(packed_resid, "dp", axis=1, tiled=True),
    )
    where_at = owner_shard * slot_count + slot_rank
    block_points = all_points[where_at]
    block_resid = all_resid[:, where_at]
    block_sq = jnp.sum(block_points * block_points, axis=1)
    inner_block = lax.dot_general(
        block_points,
        block_points,
        (((1,), (1,)), ((), ())),
        precision=highest,
        preferred_element_type=jnp.float32,
    )
    kernel_block = jnp.exp(-(block_sq[:, None] + block_sq[None, :] - 2.0 * inner_block) / mean_sq)
    system = kernel_block + ridge_weight * jnp.eye(BLOCK, dtype=jnp.float32)
    factor = jnp.linalg.cholesky(system)
    increment = jax.scipy.linalg.cho_solve((factor, True), block_resid.T).T
    model_count = lax.axis_size("mp")
    column_count = BLOCK // model_count
    start_col = lax.axis_index("mp") * column_count
    centers = lax.dynamic_slice_in_dim(block_points, start_col, column_count, 0)
    center_sq = lax.dynamic_slice_in_dim(block_sq, start_col, column_count, 0)
    inner = lax.dot_general(
        centers,
        points,
        (((1,), (1,)), ((), ())),
        precision=highest,
        preferred_element_type=jnp.float32,
    )
    weights = jnp.exp(-(center_sq[:, None] + own_squares[None, :] - 2.0 * inner) / mean_sq)
    all_increment = lax.all_gather(increment, "mp", axis=0, tiled=True)
    increment_cols = lax.dynamic_slice_in_dim(all_increment, start_col, column_count, 1)
    change = lax.psum_scatter(
        jnp.dot(increment_cols, weights, precision=highest, preferred_element_type=jnp.float32),
        "mp",
        scatter_dimension=0,
        tiled=True,
    )
    column = jnp.where(mine, local_row, shard_rows)
    new_residual = (residual - change).at[:, column].add(-ridge_weight * increment, mode="drop")
    new_coeffs = coeffs.at[:, column].add(increment, mode="drop")
    return (new_residual, new_coeffs)


def solution(mesh):
    placed = (P("dp", None), P("mp", "dp"), P("mp", "dp"), P())
    return jax.shard_map(
        on_device,
        mesh=mesh,
        in_specs=placed,
        out_specs=(P("mp", "dp"), P("mp", "dp")),
        check_vma=False,
    )
```

profile of v0, /device:TPU:24, one launch (start us, length us, event | category | flops | bytes accessed | tf_op | source)
XLA Modules:
  0.0 601.2 jit_solution(8872869057403850764)
XLA Ops:
  8.9 22.4 %scatter_custom_fusion = f32[16,256]{1,0:T(8,128)} fusion(s32[512]{0:T(512)S(1)} %get-tuple-element.45, f32[2048,256]{1,0:T(8,128)} %param.4, s32[1024]{0:T(1024)S(1)} %pad_clamp_fusion.1, f32[]{:T(128)} %constant.179.clone.1), kind=kCustom, calls=%fused_computation.41 | custom fusion | bytes 16896 | tf_op jit(solution)/shard_map/scatter | solution.py:38
  31.3 2.7 multiply_reduce_fusion
  34.1 218.1 %psum.7 = f32[]{:T(128)} all-reduce(f32[]{:T(128)} %get-tuple-element.15), channel_id=1, replica_groups=mesh['dp'=128,'mp'=4] {'dp'}, use_global_device_ids=true, to_apply=%region_4.5 | all-reduce | flops 1 | bytes 8 | tf_op jit(solution)/shard_map/psum | solution.py:24
  252.5 3.2 scatter_custom_fusion.1
  256.4 139.2 %all_gather.10 = f32[32,2048]{0,1:T(8,128)S(1)} all-gather(f32[32,16]{0,1:T(8,128)S(1)} %scatter_custom_fusion.1), channel_id=1, replica_groups=mesh['dp'=128,'mp'=4] {'dp'}, dimensions={1}, use_global_device_ids=true | all-gather | bytes 264192 | tf_op jit(solution)/shard_map/all_gather | solution.py:47
  396.7 3.2 gather_fusion
  400.0 2.5 broadcast_add_fusion
  404.1 2.6 copy.16
  406.7 1.6 add_multiply_fusion
  409.3 11.7 %cholesky.104 = f32[128,128]{1,0:T(8,128)S(1)} custom-call(f32[128,128]{1,0:T(8,128)S(1)} %cholesky.266), custom_call_target="Cholesky" | custom-call | tf_op jit(solution)/shard_map/jit(cholesky)/cholesky | solution.py:62
  421.2 9.8 %custom-call.34 = f32[1,128,128]{1,2,0:T(8,128)S(1)} custom-call(f32[1,128,128]{2,1,0:T(8,128)S(1)} %get-tuple-element.40), custom_call_target="InvertDiagBlocksLowerTriangular" | custom-call | tf_op jit(solution)/shard_map/jit(cholesky)/cholesky | solution.py:62
  433.5 12.1 %cholesky.217 = f32[128,128]{1,0:T(8,128)S(1)} custom-call(f32[128,128]{1,0:T(8,128)S(1)} %cholesky.270), custom_call_target="Cholesky" | custom-call | tf_op jit(solution)/shard_map/jit(cholesky)/cholesky | solution.py:62
  445.7 9.8 %custom-call.35 = f32[1,128,128]{1,2,0:T(8,128)S(1)} custom-call(f32[1,128,128]{2,1,0:T(8,128)S(1)} %get-tuple-element.37), custom_call_target="InvertDiagBlocksLowerTriangular" | custom-call | tf_op jit(solution)/shard_map/jit(cholesky)/cholesky | solution.py:62
  457.1 11.7 %cholesky.238 = f32[128,128]{1,0:T(8,128)S(1)} custom-call(f32[128,128]{1,0:T(8,128)S(1)} %cholesky.275), custom_call_target="Cholesky" | custom-call | tf_op jit(solution)/shard_map/jit(cholesky)/cholesky | solution.py:62
  469.5 9.8 %custom-call.36 = f32[1,128,128]{1,2,0:T(8,128)S(1)} custom-call(f32[1,128,128]{2,1,0:T(8,128)S(1)} %get-tuple-element.34), custom_call_target="InvertDiagBlocksLowerTriangular" | custom-call | tf_op jit(solution)/shard_map/jit(cholesky)/cholesky | solution.py:62
  480.8 11.9 %cholesky.255 = f32[128,128]{1,0:T(8,128)S(1)} custom-call(f32[128,128]{1,0:T(8,128)S(1)} %convolution_subtract_fusion.5), custom_call_target="Cholesky" | custom-call | tf_op jit(solution)/shard_map/jit(cholesky)/cholesky | solution.py:62
  496.7 8.0 %while.1 = (s32[]{:T(128)}, f32[512,512]{1,0:T(8,128)S(1)}, s32[4,2]{0,1:T(2,128)S(1)}, f32[4,128,128]{2,1,0:T(8,128)S(1)}, s32[]{:T(128)}) while((s32[]{:T(128)}, f32[512,512]{1,0:T(8,128)S(1)}, s32[4,2]{0,1:T(2,128)S(1)}, f32[4,128,128]{2,1,0:T(8,128)S(1)}, s32[]{:T(128)}) %tuple.41), condition=%wide.while_cond, body=%wide.while_body.sunk | while | flops 2 | bytes 131181 | solution.py:63
  504.7 39.3 %custom-call.37 = f32[4,128,128]{1,2,0:T(8,128)S(1)} custom-call(f32[4,128,128]{2,1,0:T(8,128)S(1)} %get-tuple-element.9), custom_call_target="InvertDiagBlocksLowerTriangular" | custom-call | tf_op jit(solution)/shard_map/jit(_cho_solve)/triangular_solve | solution.py:63
  547.4 12.7 %all_gather.11 = f32[128,512]{1,0:T(8,128)S(1)} all-gather(f32[32,512]{1,0:T(8,128)S(1)} %get-tuple-element.30), channel_id=1, replica_groups=mesh['dp'=128,'mp'=4] {'mp'}, dimensions={0}, use_global_device_ids=true | all-gather | bytes 327680 | tf_op jit(solution)/shard_map/all_gather | solution.py:77
  560.2 2.3 fusion.3
  562.5 2.0 fusion.30
  565.2 3.7 scatter_fusion.1
  569.9 18.0 %reduce-scatter.2.cloned.1.call-done = f32[32,2048]{1,0:T(8,128)} async-done(((f32[128,2048]{1,0:T(8,128)}), f32[32,2048]{1,0:T(8,128)}) %reduce-scatter.2.cloned.1.call-update) | async-done | bytes 262160 | tf_op jit(solution)/shard_map/reduce_scatter | solution.py:79
  589.2 3.9 scatter_fusion
  (79 shorter events, 29.0 us)
Async XLA Ops:
  7.2 245.0 %copy-start.2 = (f32[32,2048]{1,0:T(8,128)S(1)}, f32[32,2048]{1,0:T(8,128)}, u32[]{:S(2)}) copy-start(f32[32,2048]{1,0:T(8,128)} %param.5) | copy-start | bytes 786436
  7.2 389.5 %all-gather.2.cloned.1.call-start = ((), (), s32[]{:S(2)}) async-start(), calls=%async_computation.1 | async-start | bytes 2113536 | tf_op jit(solution)/shard_map/all_gather | solution.py:46
  31.3 556.6 %reduce-scatter.2.cloned.1.call-start = ((), (), s32[]{:S(2)}) async-start(), calls=%async_computation.2 | async-start | bytes 1310720 | tf_op jit(solution)/shard_map/reduce_scatter | solution.py:79
  408.3 1.0 copy-start
  544.0 16.2 %copy-start.1 = (f32[2048,256]{1,0:T(8,128)S(1)}, f32[2048,256]{1,0:T(8,128)}, u32[]{:S(2)}) copy-start(f32[2048,256]{1,0:T(8,128)} %param.4) | copy-start | bytes 6291460
  562.5 2.1 copy-start.3
Sparse Core Ops, SparseCore 0:
  31.4 143.9 all-gather.1
  564.7 23.1 reduce-scatter.1
where the time goes:
time: 608 us; the launch traced here: 601 us
  blocking collectives  370 us (61%)
  other arithmetic  133 us (22%)
  local copies, waits for them, and re-layouts  46.3 us (8%)
  waiting for transfers between devices  18.1 us (3%)
  between operations  17.9 us (3%)
  matrix products  15.6 us (3%)
    psum x1, blocking collectives, on_device(): square_total = lax.psum(jnp.sum(own_squares), 'dp')  218 us
    all_gather x1, blocking collectives, on_device(): lax.all_gather(packed_resid, 'dp', axis=1, tiled=True)  139 us
    another operation x14, other arithmetic, on_device(): factor = jnp.linalg.cholesky(system)  79 us
    another operation x4, other arithmetic, on_device(): increment = jax.scipy.linalg.cho_solve((factor, True), block_resid.T).T  39.5 us
    scatter x1, local copies, waits for them, and re-layouts, on_device(): packed_points = jnp.zeros((slot_count, feature_count), jnp.float32).at[sl...  22.4 us
    reduce_scatter x1, waiting for transfers between devices, on_device(): lax.psum_scatter(jnp.dot(increment_cols, weights, precision=highest, pref...  18 us
    all_gather x1, blocking collectives, on_device(): all_increment = lax.all_gather(increment, 'mp', axis=0, tiled=True)  12.7 us
  transfers between devices with their start and end apart: 2, of which 1 were waited for; matrix products, arithmetic and copies ran while one was open for 2% of the time, Pallas kernels for 0%

commit v1 on v0

v1 whole, which is shorter than its diff:
```python
import jax
import jax.numpy as jnp
from jax import lax
from jax.sharding import PartitionSpec as P

BLOCK = 512


ridge_weight = 1.0


def on_device(points, residual, coeffs, block_index):
    highest = lax.Precision.HIGHEST
    shard_rows = points.shape[0]
    feature_count = points.shape[1]
    output_rows = residual.shape[0]
    dp_count = lax.axis_size("dp")
    position = lax.axis_index("dp")
    owner_shard = block_index // shard_rows
    local_row = block_index - owner_shard * shard_rows
    mine = owner_shard == position
    safe_row = jnp.where(mine, local_row, 0)
    own_squares = jnp.sum(points * points, axis=1)
    own_total = jnp.sum(own_squares)
    picked_points = jnp.where(mine[:, None], points[safe_row], 0.0)
    picked_resid = jnp.where(mine[:, None], residual[:, safe_row].T, 0.0)
    body = jnp.concatenate([picked_points, picked_resid], axis=1)
    extra = jnp.zeros((8, feature_count + output_rows), jnp.float32).at[0, 0].set(own_total)
    packed = jnp.concatenate([body, extra], axis=0)
    summed = lax.psum(packed, "dp")
    block_points = summed[:BLOCK, :feature_count]
    block_resid = summed[:BLOCK, feature_count:].T
    mean_sq = summed[BLOCK, 0] / (shard_rows * dp_count)
    block_sq = jnp.sum(block_points * block_points, axis=1)
    inner_block = lax.dot_general(
        block_points,
        block_points,
        (((1,), (1,)), ((), ())),
        precision=highest,
        preferred_element_type=jnp.float32,
    )
    kernel_block = jnp.exp(-(block_sq[:, None] + block_sq[None, :] - 2.0 * inner_block) / mean_sq)
    system = kernel_block + ridge_weight * jnp.eye(BLOCK, dtype=jnp.float32)
    factor = jnp.linalg.cholesky(system)
    increment = jax.scipy.linalg.cho_solve((factor, True), block_resid.T).T
    inner = lax.dot_general(
        block_points,
        points,
        (((1,), (1,)), ((), ())),
        precision=highest,
        preferred_element_type=jnp.float32,
    )
    weights = jnp.exp(-(block_sq[:, None] + own_squares[None, :] - 2.0 * inner) / mean_sq)
    change = jnp.dot(increment, weights, precision=highest, preferred_element_type=jnp.float32)
    column = jnp.where(mine, local_row, shard_rows)
    new_residual = (residual - change).at[:, column].add(-ridge_weight * increment, mode="drop")
    new_coeffs = coeffs.at[:, column].add(increment, mode="drop")
    return (new_residual, new_coeffs)


def solution(mesh):
    placed = (P("dp", None), P("mp", "dp"), P("mp", "dp"), P())
    return jax.shard_map(
        on_device,
        mesh=mesh,
        in_specs=placed,
        out_specs=(P("mp", "dp"), P("mp", "dp")),
        check_vma=False,
    )
```

time: 608 us -> 575 us (0.946)
  the two profiles are of different devices: /device:TPU:24 before, /device:TPU:2 now
where the time goes in v1:
time: 575 us; the launch traced here: 564 us
  waiting for transfers between devices  342 us (59%)
  other arithmetic  142 us (25%)
  local copies, waits for them, and re-layouts  32.6 us (6%)
  matrix products  29.7 us (5%)
  between operations  17.9 us (3%)
    psum x1, waiting for transfers between devices, on_device(): summed = lax.psum(packed, 'dp')  342 us
    another operation x14, other arithmetic, on_device(): factor = jnp.linalg.cholesky(system)  80.9 us
    another operation x4, other arithmetic, on_device(): increment = jax.scipy.linalg.cho_solve((factor, True), block_resid.T).T  42.5 us
    another operation x12, local copies, waits for them, and re-layouts  14.5 us
  transfers between devices with their start and end apart: 1, of which 1 were waited for; matrix products, arithmetic and copies ran while one was open for 0% of the time, Pallas kernels for 0%

profile of v1, /device:TPU:2, one launch (start us, length us, event | category | flops | bytes accessed | tf_op | source)
XLA Modules:
  0.0 564.3 jit_solution(12896073595345260882)
XLA Ops:
  10.6 2.8 multiply_reduce_fusion
  20.9 341.7 %all-reduce.4.cloned.1.call-done = f32[520,288]{1,0:T(8,128)} async-done(((f32[520,288]{1,0:T(8,128)}), f32[520,288]{1,0:T(8,128)}) %all-reduce.4.cloned.1.call-update) | async-done | bytes 599056 | tf_op jit(solution)/shard_map/psum | solution.py:30
  364.4 4.0 broadcast_add_fusion
  368.4 2.6 copy.7
  371.0 2.5 copy.8
  375.3 2.3 add_multiply_fusion
  378.6 11.7 %cholesky.104 = f32[128,128]{1,0:T(8,128)S(1)} custom-call(f32[128,128]{1,0:T(8,128)S(1)} %cholesky.266), custom_call_target="Cholesky" | custom-call | tf_op jit(solution)/shard_map/jit(cholesky)/cholesky | solution.py:44
  391.5 9.8 %custom-call.34 = f32[1,128,128]{1,2,0:T(8,128)S(1)} custom-call(f32[1,128,128]{2,1,0:T(8,128)S(1)} %get-tuple-element.49), custom_call_target="InvertDiagBlocksLowerTriangular" | custom-call | tf_op jit(solution)/shard_map/jit(cholesky)/cholesky | solution.py:44
  404.6 12.2 %cholesky.217 = f32[128,128]{1,0:T(8,128)S(1)} custom-call(f32[128,128]{1,0:T(8,128)S(1)} %cholesky.270), custom_call_target="Cholesky" | custom-call | tf_op jit(solution)/shard_map/jit(cholesky)/cholesky | solution.py:44
  417.4 9.8 %custom-call.35 = f32[1,128,128]{1,2,0:T(8,128)S(1)} custom-call(f32[1,128,128]{2,1,0:T(8,128)S(1)} %get-tuple-element.46), custom_call_target="InvertDiagBlocksLowerTriangular" | custom-call | tf_op jit(solution)/shard_map/jit(cholesky)/cholesky | solution.py:44
  429.6 11.7 %cholesky.238 = f32[128,128]{1,0:T(8,128)S(1)} custom-call(f32[128,128]{1,0:T(8,128)S(1)} %cholesky.275), custom_call_target="Cholesky" | custom-call | tf_op jit(solution)/shard_map/jit(cholesky)/cholesky | solution.py:44
  442.6 9.8 %custom-call.36 = f32[1,128,128]{1,2,0:T(8,128)S(1)} custom-call(f32[1,128,128]{2,1,0:T(8,128)S(1)} %get-tuple-element.43), custom_call_target="InvertDiagBlocksLowerTriangular" | custom-call | tf_op jit(solution)/shard_map/jit(cholesky)/cholesky | solution.py:44
  454.7 11.9 %cholesky.255 = f32[128,128]{1,0:T(8,128)S(1)} custom-call(f32[128,128]{1,0:T(8,128)S(1)} %convolution_subtract_fusion.5), custom_call_target="Cholesky" | custom-call | tf_op jit(solution)/shard_map/jit(cholesky)/cholesky | solution.py:44
  471.1 2.4 select_select_fusion
  473.4 14.5 %while.2 = (s32[]{:T(128)}, f32[512,512]{1,0:T(8,128)}, s32[4,2]{0,1:T(2,128)S(1)}, f32[4,128,128]{2,1,0:T(8,128)}, s32[]{:T(128)}) while((s32[]{:T(128)}, f32[512,512]{1,0:T(8,128)}, s32[4,2]{0,1:T(2,128)S(1)}, f32[4,128,128]{2,1,0:T(8,128)}, s32[]{:T(128)}) %tuple.41), condition=%wide.while_cond.1, body=%wide.while_body.1.sunk | while | flops 2 | bytes 132705 | solution.py:45
  474.1 3.0 bitcast_dynamic-update-slice_fusion.2
  477.7 3.0 bitcast_dynamic-update-slice_fusion.2
  481.4 3.0 bitcast_dynamic-update-slice_fusion.2
  485.0 2.9 bitcast_dynamic-update-slice_fusion.2
  487.9 40.1 %custom-call.37 = f32[4,128,128]{1,2,0:T(8,128)S(1)} custom-call(f32[4,128,128]{2,1,0:T(8,128)} %get-tuple-element.21), custom_call_target="InvertDiagBlocksLowerTriangular" | custom-call | tf_op jit(solution)/shard_map/jit(_cho_solve)/triangular_solve | solution.py:45
  538.5 4.0 scatter_fusion.1
  543.7 4.9 fusion.15
  548.7 3.5 fusion.7
  552.5 3.7 scatter_fusion
  (88 shorter events, 43.3 us)
Async XLA Ops:
  7.2 6.2 %copy-start = (f32[2048,256]{1,0:T(8,128)S(1)}, f32[2048,256]{1,0:T(8,128)}, u32[]{:S(2)}) copy-start(f32[2048,256]{1,0:T(8,128)} %param.6) | copy-start | bytes 6291460
  7.2 355.5 %all-reduce.4.cloned.1.call-start = ((), (), s32[]{:S(2)}) async-start(), calls=%async_computation | async-start | bytes 1597440 | tf_op jit(solution)/shard_map/psum | solution.py:30
  363.8 0.6 copy-start.10
  377.6 1.0 copy-start.1
  535.0 2.8 copy-start.3
  536.3 1.5 copy-start.5
  537.7 0.6 copy-start.7
  542.5 6.2 %copy-start.2 = (f32[32,2048]{1,0:T(8,128)S(1)}, f32[32,2048]{1,0:T(8,128)}, u32[]{:S(2)}) copy-start(f32[32,2048]{1,0:T(8,128)} %param.7) | copy-start | bytes 786436
  542.5 6.2 %copy-start.4 = (f32[128,32]{0,1:T(8,128)S(1)}, f32[128,32]{0,1:T(8,128)}, u32[]{:S(2)}) copy-start(f32[128,32]{0,1:T(8,128)} %copy-done.3) | copy-start | bytes 49156
  542.5 6.2 %copy-start.6 = (f32[128,32]{0,1:T(8,128)S(1)}, f32[128,32]{0,1:T(8,128)}, u32[]{:S(2)}) copy-start(f32[128,32]{0,1:T(8,128)} %copy-done.5) | copy-start | bytes 49156
  542.5 6.2 %copy-start.8 = (f32[128,32]{0,1:T(8,128)S(1)}, f32[128,32]{0,1:T(8,128)}, u32[]{:S(2)}) copy-start(f32[128,32]{0,1:T(8,128)} %copy-done.7) | copy-start | bytes 49156
  542.5 6.2 %copy-start.11 = (f32[512]{0:T(512)S(1)}, f32[512]{0:T(512)}, u32[]{:S(2)}) copy-start(f32[512]{0:T(512)} %copy-done.10) | copy-start | bytes 6148
  542.5 6.2 %copy-start.12 = (f32[2048]{0:T(1024)S(1)}, f32[2048]{0:T(1024)}, u32[]{:S(2)}) copy-start(f32[2048]{0:T(1024)} %get-tuple-element.24) | copy-start | bytes 24580
  548.7 3.8 copy-start.9
Sparse Core Ops, SparseCore 0:
  19.7 342.8 all-reduce.3
